TPU v7x, 32 devices: a whole 2x2x4 slice. The times are simulated.
32 devices in a mesh: ctx: 4 (over y, core), ep: 8 (over z, x).
Axes of the slice: x: 2, y: 2, z: 4, core: 2. Of those that a mesh axis runs over, the one named last changes fastest.
Arguments:
- hidden_state: bfloat16 [512, 2048], P(('ctx', 'ep')), may hold values from -200 to 200
- upstream_grad: bfloat16 [512, 2048], P(('ctx', 'ep')), may hold values from -6 to 6
- route_ids: int32 [512, 6], P(('ctx', 'ep')), may hold values from 0 to 31, all different within a row; in each aligned block of 16 rows (0 to 15, 16 to 31, ...) at most 6 rows name the same one
- route_gates: float32 [512, 6], P(('ctx', 'ep')), may hold values from 0.05 to 0.5
- norm_gain: float32 [2048], replicated, may hold values from 0.25 to 1.75
- w_gate: bfloat16 [8, 4, 1408, 2048], P('ep', 'ctx'), may hold values from -0.125 to 0.125
- w_up: bfloat16 [8, 4, 1408, 2048], P('ep', 'ctx'), may hold values from -0.125 to 0.125
- w_down: bfloat16 [8, 4, 1408, 2048], P('ep', 'ctx'), may hold values from -0.15625 to 0.15625
- out_proj: bfloat16 [2048, 2048], P('ep'), may hold values from -0.125 to 0.125
- queries: bfloat16 [512, 2048], P('ctx', 'ep'), may hold values from -12 to 12
- key_rows: bfloat16 [512, 2048], P('ctx', 'ep'), may hold values from -12 to 12
- value_rows: bfloat16 [512, 2048], P('ctx', 'ep'), may hold values from -6 to 6
Outputs:
- grad_state: bfloat16 [512, 2048], P(('ctx', 'ep'))
- grad_queries: bfloat16 [512, 2048], P('ctx', 'ep')
- grad_keys: bfloat16 [512, 2048], P('ctx', 'ep')
- grad_values: bfloat16 [512, 2048], P('ctx', 'ep')
- grad_gate: bfloat16 [8, 4, 1408, 2048], P('ep', 'ctx')
- grad_up: bfloat16 [8, 4, 1408, 2048], P('ep', 'ctx')
- grad_down: bfloat16 [8, 4, 1408, 2048], P('ep', 'ctx')
Inputs may be any that keep to these rules, and one draw needn't show every extreme that they name: `route_ids`: within the 16 tokens of one routing block no expert is named by more than 6 routes, a bound that some block reaches.
All inputs are finite; a program needn't handle non-finite values.
Results may differ from a plain program's by a relative error of at most 0.015.
Values may be sent and summed in bfloat16 or wider, within the bound.
No kernel may reach another device: no remote copies, remote signals or barrier semaphores. Data moves between devices by JAX's collectives and lax.ppermute only.
A program may use at most 128 MiB of HBM per device.

v0:
```python
import math
import jax
import jax.numpy as jnp
from jax import lax
from jax.sharding import PartitionSpec as P

HD = 128
EXP_DEV = 4
EPSILON = 1e-06
FLOOR_SCORE = -1e30
PRECISE = lax.Precision.HIGHEST


def shifted(block, axis, distance):
    devices = range(lax.axis_size(axis))
    route = [((i - distance) % len(devices), i) for i in devices]
    return lax.ppermute(block, axis, route)


def expert_pass(token_rows, grad_rows, gate_rows, up_rows, down_rows):
    contract = (((1,), (1,)), ((), ()))
    over_rows = (((0,), (0,)), ((), ()))
    pre_gate = lax.dot_general(token_rows, gate_rows, contract, preferred_element_type=jnp.float32)
    up_value = lax.dot_general(token_rows, up_rows, contract, preferred_element_type=jnp.float32)
    sigmoid = jax.nn.sigmoid(pre_gate)
    activation = (pre_gate * sigmoid * up_value).astype(jnp.bfloat16)
    act_grad = lax.dot_general(grad_rows, down_rows, contract, preferred_element_type=jnp.float32)
    up_grad = (act_grad * pre_gate * sigmoid).astype(jnp.bfloat16)
    gate_grad = (act_grad * up_value * sigmoid * (1.0 + pre_gate * (1.0 - sigmoid))).astype(
        jnp.bfloat16
    )
    partial_value = (
        jnp.dot(gate_grad, gate_rows, preferred_element_type=jnp.float32)
        + jnp.dot(up_grad, up_rows, preferred_element_type=jnp.float32)
    ).astype(jnp.bfloat16)
    gate_total = lax.dot_general(
        gate_grad, token_rows, over_rows, preferred_element_type=jnp.float32
    )
    up_total = lax.dot_general(up_grad, token_rows, over_rows, preferred_element_type=jnp.float32)
    down_total = lax.dot_general(
        activation, grad_rows, over_rows, preferred_element_type=jnp.float32
    )
    return (partial_value, gate_total, up_total, down_total)


def score_tile(query_heads, key_heads, query_first, key_first):
    scale = 1.0 / math.sqrt(query_heads.shape[2])
    raw_scores = (
        jnp.einsum("qhd,khd->hqk", query_heads, key_heads, preferred_element_type=jnp.float32)
        * scale
    )
    query_pos = query_first + jnp.arange(query_heads.shape[0], dtype=jnp.int32)
    key_pos = key_first + jnp.arange(key_heads.shape[0], dtype=jnp.int32)
    return (raw_scores, (query_pos[:, None] >= key_pos[None, :])[None, :, :])


def stats_update(state_carry, key_part, value_part, key_first, query_heads, query_first):
    row_top, row_total, weighted = state_carry
    head_count, head_size = (query_heads.shape[1], query_heads.shape[2])
    key_heads = key_part.reshape(-1, head_count, head_size)
    value_heads = value_part.reshape(-1, head_count, head_size)
    raw_scores, allowed = score_tile(query_heads, key_heads, query_first, key_first)
    new_top = jnp.maximum(row_top, jnp.max(jnp.where(allowed, raw_scores, FLOOR_SCORE), axis=2))
    weights = jnp.where(allowed, jnp.exp(raw_scores - new_top[:, :, None]), 0.0)
    row_total = jnp.sum(weights, axis=2)
    weighted = jnp.einsum(
        "hqk,khd->hqd", weights, value_heads.astype(jnp.float32), precision=PRECISE
    )
    return (new_top, row_total, weighted)


def tile_grads(
    key_part, value_part, key_first, query_heads, dout_heads, log_total, row_delta, query_first
):
    head_count, head_size = (query_heads.shape[1], query_heads.shape[2])
    scale = 1.0 / math.sqrt(head_size)
    key_heads = key_part.reshape(-1, head_count, head_size)
    value_heads = value_part.reshape(-1, head_count, head_size)
    raw_scores, allowed = score_tile(query_heads, key_heads, query_first, key_first)
    probs = jnp.where(allowed, jnp.exp(raw_scores - log_total[:, :, None]), 0.0)
    value_grad = jnp.einsum(
        "hqk,qhd->khd", probs.astype(jnp.bfloat16), dout_heads, preferred_element_type=jnp.float32
    )
    prob_grad = jnp.einsum(
        "qhd,khd->hqk", dout_heads, value_heads, preferred_element_type=jnp.float32
    )
    score_grad = (probs * (prob_grad - row_delta[:, :, None])).astype(jnp.bfloat16)
    query_grad = (
        jnp.einsum("hqk,khd->qhd", score_grad, key_heads, preferred_element_type=jnp.float32)
        * scale
    )
    key_grad = (
        jnp.einsum("hqk,qhd->khd", score_grad, query_heads, preferred_element_type=jnp.float32)
        * scale
    )
    return (query_grad, key_grad, value_grad)


def local(
    hidden_state,
    upstream_grad,
    route_ids,
    route_gates,
    norm_gain,
    w_gate,
    w_up,
    w_down,
    out_proj,
    queries,
    key_rows,
    value_rows,
):
    ep_count = lax.axis_size("ep")
    ctx_count = lax.axis_size("ctx")
    tok_dev, model_width = hidden_state.shape
    topk_count = route_ids.shape[1]
    expert_count = EXP_DEV * ep_count
    copies = ctx_count // EXP_DEV
    capacity = max(2, 2 * tok_dev * topk_count // expert_count)
    route_count = tok_dev * topk_count
    tok_ctx = queries.shape[0]
    head_count = queries.shape[1] // HD
    ctx_index = lax.axis_index("ctx")
    query_first = ctx_index * tok_ctx
    query_heads = queries.reshape(tok_ctx, head_count, HD)
    stats_init = (
        jnp.full((head_count, tok_ctx), FLOOR_SCORE, jnp.float32),
        jnp.zeros((head_count, tok_ctx), jnp.float32),
        jnp.zeros((head_count, tok_ctx, HD), jnp.float32),
    )
    softmax_stats = stats_update(
        stats_init,
        lax.all_gather(key_rows, "ctx", axis=0, tiled=True),
        lax.all_gather(value_rows, "ctx", axis=0, tiled=True),
        jnp.int32(0),
        query_heads,
        query_first,
    )
    state = hidden_state.astype(jnp.float32)
    inv_rms = lax.rsqrt(jnp.mean(state * state, axis=1, keepdims=True) + EPSILON)
    normed = (state * inv_rms * norm_gain[None, :]).astype(jnp.bfloat16)
    flat_ids = route_ids.reshape(route_count)
    matches = (flat_ids[:, None] == jnp.arange(expert_count, dtype=jnp.int32)[None, :]).astype(
        jnp.int32
    )
    earlier = jnp.cumsum(matches, axis=0) - matches
    slot_index = jnp.sum(earlier * matches, axis=1)
    slot_ids = jnp.arange(capacity, dtype=jnp.int32)
    dispatch = (
        matches.T[:, None, :] * (slot_index[None, None, :] == slot_ids[None, :, None])
    ).astype(jnp.bfloat16)
    dispatch = dispatch.reshape(ep_count, EXP_DEV, capacity, route_count)
    normed_rep = jnp.repeat(normed, topk_count, axis=0)
    upstream_rep = jnp.repeat(upstream_grad, topk_count, axis=0).astype(jnp.float32)
    scaled_grads = (route_gates.reshape(route_count, 1) * upstream_rep).astype(jnp.bfloat16)
    gate_w = w_gate[0, 0]
    up_w = w_up[0, 0]
    down_w = w_down[0, 0]
    send_rows = jnp.repeat(
        jnp.einsum(
            "jecr,rd->jecd", dispatch, normed_rep, preferred_element_type=jnp.float32
        ).astype(jnp.bfloat16),
        copies,
        axis=1,
    )
    send_grads = jnp.repeat(
        jnp.einsum(
            "jecr,rd->jecd", dispatch, scaled_grads, preferred_element_type=jnp.float32
        ).astype(jnp.bfloat16),
        copies,
        axis=1,
    )
    received = (
        lax.all_to_all(send_rows, "ep", split_axis=0, concat_axis=0, tiled=True),
        lax.all_to_all(send_grads, "ep", split_axis=0, concat_axis=0, tiled=True),
    )
    received = (
        lax.all_to_all(received[0], "ctx", split_axis=1, concat_axis=1, tiled=True),
        lax.all_to_all(received[1], "ctx", split_axis=1, concat_axis=1, tiled=True),
    )
    partial_value, gate_total, up_total, down_total = expert_pass(
        received[0].reshape(-1, model_width),
        received[1].reshape(-1, model_width),
        gate_w,
        up_w,
        down_w,
    )
    returned = lax.all_to_all(
        partial_value.reshape(ep_count, ctx_count, capacity, model_width),
        "ctx",
        split_axis=1,
        concat_axis=1,
        tiled=True,
    )
    returned = lax.all_to_all(returned, "ep", split_axis=0, concat_axis=0, tiled=True)
    summed = jnp.sum(
        returned.reshape(ep_count, EXP_DEV, copies, capacity, model_width).astype(jnp.float32),
        axis=2,
    )
    d_routes = jnp.einsum("jecd,jecr->rd", summed, dispatch.astype(jnp.float32), precision=PRECISE)
    d_normed = jnp.sum(d_routes.reshape(tok_dev, topk_count, model_width), axis=1)
    scaled_norm = norm_gain[None, :] * d_normed
    projection = jnp.mean(state * scaled_norm, axis=1, keepdims=True)
    grad_state = (
        upstream_grad.astype(jnp.float32)
        + inv_rms * scaled_norm
        - state * inv_rms * inv_rms * inv_rms * projection
    ).astype(jnp.bfloat16)
    dout = lax.dot_general(
        lax.all_gather(grad_state, "ep", axis=0, tiled=True),
        out_proj,
        (((1,), (1,)), ((), ())),
        preferred_element_type=jnp.float32,
    ).astype(jnp.bfloat16)
    dout_heads = dout.reshape(tok_ctx, head_count, HD)
    row_top, row_total, weighted = softmax_stats
    log_total = row_top + jnp.log(row_total)
    attn_out = weighted / row_total[:, :, None]
    row_delta = jnp.einsum(
        "qhd,hqd->hq", dout_heads.astype(jnp.float32), attn_out, precision=PRECISE
    )
    query_zero = jnp.zeros((tok_ctx, head_count, HD), jnp.float32)

    def cycle_turn(turn_index, cycle_carry):
        query_pair, moving_grad, moving_stats, key_value_acc = cycle_carry
        source_dev = (ctx_index - turn_index) % ctx_count
        query_part, key_part, value_part = tile_grads(
            key_rows,
            value_rows,
            query_first,
            query_pair[0],
            query_pair[1],
            moving_stats[0],
            moving_stats[1],
            source_dev * tok_ctx,
        )
        key_value_acc = key_value_acc + jnp.stack([key_part, value_part])
        moving_grad = moving_grad + query_part
        query_pair = shifted(query_pair, "ctx", 1)
        moving_grad, moving_stats = shifted((moving_grad, moving_stats), "ctx", 1)
        return (query_pair, moving_grad, moving_stats, key_value_acc)

    query_pair_init = jnp.stack([query_heads, dout_heads])
    stats_pair = jnp.stack([log_total, row_delta])
    acc_init = jnp.zeros((2, tok_ctx, head_count, HD), jnp.float32)
    pair_final, query_grad, stats_final, key_value_grad = lax.fori_loop(
        0, ctx_count, cycle_turn, (query_pair_init, query_zero, stats_pair, acc_init)
    )
    flat_width = head_count * HD
    grad_queries = query_grad.reshape(tok_ctx, flat_width).astype(jnp.bfloat16)
    grad_keys = key_value_grad[0].reshape(tok_ctx, flat_width).astype(jnp.bfloat16)
    grad_values = key_value_grad[1].reshape(tok_ctx, flat_width).astype(jnp.bfloat16)
    return (
        grad_state,
        grad_queries,
        grad_keys,
        grad_values,
        gate_total.astype(jnp.bfloat16)[None, None],
        up_total.astype(jnp.bfloat16)[None, None],
        down_total.astype(jnp.bfloat16)[None, None],
    )


def solution(mesh):
    placed = (
        P(("ctx", "ep"), None),
        P(("ctx", "ep"), None),
        P(("ctx", "ep"), None),
        P(("ctx", "ep"), None),
        P(),
        P("ep", "ctx", None, None),
        P("ep", "ctx", None, None),
        P("ep", "ctx", None, None),
        P("ep", None),
        P("ctx", "ep"),
        P("ctx", "ep"),
        P("ctx", "ep"),
    )
    return jax.shard_map(
        local,
        mesh=mesh,
        in_specs=placed,
        out_specs=(
            P(("ctx", "ep"), None),
            P("ctx", "ep"),
            P("ctx", "ep"),
            P("ctx", "ep"),
            P("ep", "ctx", None, None),
            P("ep", "ctx", None, None),
            P("ep", "ctx", None, None),
        ),
        check_vma=False,
    )
```

profile of v0, /device:TPU:0, one launch (start us, length us, event | category | flops | bytes accessed | tf_op | source)
XLA Modules:
  0.0 223.2 jit_solution(10638249920993625415)
XLA Ops:
  4.6 1.5 copy.110
  6.1 7.3 %all-to-all-start.2 = ((bf16[8,4,6,2048]{3,1,2,0:T(4,128)(2,1)}), bf16[8,4,6,2048]{3,1,2,0:T(4,128)(2,1)}, u32[]{:S(2)}, u32[]{:S(2)}) async-start(bf16[8,4,6,2048]{3,1,2,0:T(4,128)(2,1)} %copy.110), calls=%async_computation.2 | async-start | bytes 1572864 | tf_op jit(solution)/shard_map/all_to_all | solution.py:174
  14.2 1.5 copy.107
  15.7 17.9 %all-to-all-done.2 = bf16[8,4,6,2048]{3,1,2,0:T(4,128)(2,1)} async-done(((bf16[8,4,6,2048]{3,1,2,0:T(4,128)(2,1)}), bf16[8,4,6,2048]{3,1,2,0:T(4,128)(2,1)}, u32[]{:S(2)}, u32[]{:S(2)}) %all-to-all-start.2) | async-done | bytes 786464 | tf_op jit(solution)/shard_map/all_to_all | solution.py:174
  33.6 3.6 %all-to-all-start = ((bf16[8,4,6,2048]{3,1,2,0:T(4,128)(2,1)}), bf16[8,4,6,2048]{3,1,2,0:T(4,128)(2,1)S(1)}, u32[]{:S(2)}, u32[]{:S(2)}) async-start(bf16[8,4,6,2048]{3,1,2,0:T(4,128)(2,1)} %copy.107), calls=%async_computation | async-start | bytes 1572864 | tf_op jit(solution)/shard_map/all_to_all | solution.py:175
  37.2 2.5 %copy.111 = bf16[8,4,6,2048]{3,0,2,1:T(8,128)(2,1)} copy(bf16[8,4,6,2048]{3,1,2,0:T(4,128)(2,1)} %all-to-all-done.2) | data formatting | bytes 1572864 | tf_op jit(solution)/shard_map/all_to_all | solution.py:174
  39.7 17.9 %all-to-all-done = bf16[8,4,6,2048]{3,1,2,0:T(4,128)(2,1)S(1)} async-done(((bf16[8,4,6,2048]{3,1,2,0:T(4,128)(2,1)}), bf16[8,4,6,2048]{3,1,2,0:T(4,128)(2,1)S(1)}, u32[]{:S(2)}, u32[]{:S(2)}) %all-to-all-start) | async-done | bytes 786464 | tf_op jit(solution)/shard_map/all_to_all | solution.py:175
  57.6 3.5 %all-to-all-start.3 = ((bf16[8,4,6,2048]{3,0,2,1:T(8,128)(2,1)}), bf16[8,4,6,2048]{3,0,2,1:T(8,128)(2,1)S(1)}, u32[]{:S(2)}, u32[]{:S(2)}) async-start(bf16[8,4,6,2048]{3,0,2,1:T(8,128)(2,1)} %copy.111), calls=%async_computation.3 | async-start | bytes 1572864 | tf_op jit(solution)/shard_map/all_to_all | solution.py:178
  61.4 13.6 %all_gather.11 = bf16[512,256]{0,1:T(8,128)(2,1)S(1)} all-gather(bf16[128,256]{0,1:T(8,128)(2,1)S(1)} %copy.121), channel_id=1, replica_groups=mesh['ctx'=4,'ep'=8] {'ctx'}, dimensions={0}, use_global_device_ids=true | all-gather | bytes 327680 | tf_op jit(solution)/shard_map/all_gather | solution.py:134
  76.3 4.2 %all-to-all-start.1 = ((bf16[8,4,6,2048]{3,0,2,1:T(8,128)(2,1)}), bf16[8,4,6,2048]{3,0,2,1:T(8,128)(2,1)}, u32[]{:S(2)}, u32[]{:S(2)}) async-start(bf16[8,4,6,2048]{3,0,2,1:T(8,128)(2,1)} %copy.108), calls=%async_computation.1 | async-start | bytes 1572864 | tf_op jit(solution)/shard_map/all_to_all | solution.py:179
  80.5 13.9 %all_gather.10 = bf16[512,256]{0,1:T(8,128)(2,1)S(1)} all-gather(bf16[128,256]{0,1:T(8,128)(2,1)S(1)} %copy.118), channel_id=1, replica_groups=mesh['ctx'=4,'ep'=8] {'ctx'}, dimensions={0}, use_global_device_ids=true | all-gather | bytes 327680 | tf_op jit(solution)/shard_map/all_gather | solution.py:133
  98.0 1.6 copy.109
  100.8 4.7 %fusion.28 = f32[192,1408]{1,0:T(8,128)S(1)} fusion(bf16[192,2048]{1,0:T(8,128)(2,1)S(1)} %copy-done.6, bf16[1,1,1408,2048]{3,2,1,0:T(8,128)(2,1)} %param.19), kind=kOutput, calls=%fused_computation.42 | convolution fusion | flops 1107296256 | bytes 7634944 | tf_op jit(solution)/shard_map/dot_general | solution.py:23
  105.5 5.1 %fusion.32 = f32[192,1408]{1,0:T(8,128)S(1)} fusion(bf16[192,2048]{1,0:T(8,128)(2,1)S(1)} %copy-done.6, bf16[1,1,1408,2048]{3,2,1,0:T(8,128)(2,1)} %param.20), kind=kOutput, calls=%fused_computation.46 | convolution fusion | flops 1107296256 | bytes 7634944 | tf_op jit(solution)/shard_map/dot_general | solution.py:24
  110.7 5.3 %multiply_convert_fusion.1 = (bf16[192,1408]{1,0:T(8,128)(2,1)S(1)}, bf16[192,1408]{1,0:T(8,128)(2,1)S(1)}) fusion(f32[192,1408]{1,0:T(8,128)S(1)} %fusion.28, f32[192,1408]{1,0:T(8,128)S(1)} %fusion.32, bf16[192,2048]{1,0:T(8,128)(2,1)S(1)} %copy-done.8, bf16[1,1,1408,2048]{3,2,1,0:T(8,128)(2,1)} %param.21), kind=kOutput, calls=%fused_computation.62 | convolution fusion | flops 1110810624 | bytes 9797632 | tf_op jit(solution)/shard_map/dot_general | solution.py:27
  117.5 2.3 %fusion.39 = bf16[192,2048]{1,0:T(8,128)(2,1)} fusion(f32[192,2048]{1,0:T(8,128)S(1)} %fusion.26, bf16[192,1408]{1,0:T(8,128)(2,1)S(1)} %get-tuple-element.317, bf16[1,1,1408,2048]{3,2,1,0:T(8,128)(2,1)S(1)} %bitcast.175), kind=kOutput, calls=%fused_computation.51 | convolution fusion | flops 1108082688 | bytes 8667136 | tf_op jit(solution)/shard_map/dot_general | solution.py:34
  122.5 3.5 %all-to-all-start.4 = ((bf16[8,4,6,2048]{3,0,2,1:T(8,128)(2,1)}), bf16[8,4,6,2048]{3,0,2,1:T(8,128)(2,1)S(1)}, u32[]{:S(2)}, u32[]{:S(2)}) async-start(bf16[8,4,6,2048]{3,0,2,1:T(8,128)(2,1)} %copy.113), calls=%async_computation.4 | async-start | bytes 1572864 | tf_op jit(solution)/shard_map/all_to_all | solution.py:188
  126.3 11.3 %all-to-all-done.4 = bf16[8,4,6,2048]{3,0,2,1:T(8,128)(2,1)S(1)} async-done(((bf16[8,4,6,2048]{3,0,2,1:T(8,128)(2,1)}), bf16[8,4,6,2048]{3,0,2,1:T(8,128)(2,1)S(1)}, u32[]{:S(2)}, u32[]{:S(2)}) %all-to-all-start.4) | async-done | bytes 786464 | tf_op jit(solution)/shard_map/all_to_all | solution.py:188
  137.6 1.5 copy.114
  139.1 3.8 %all-to-all-start.5 = ((bf16[8,4,6,2048]{3,1,2,0:T(4,128)(2,1)}), bf16[8,4,6,2048]{3,1,2,0:T(4,128)(2,1)S(1)}, u32[]{:S(2)}, u32[]{:S(2)}) async-start(bf16[8,4,6,2048]{3,1,2,0:T(4,128)(2,1)} %copy.114), calls=%async_computation.5 | async-start | bytes 1572864 | tf_op jit(solution)/shard_map/all_to_all | solution.py:195
  143.0 5.6 %fusion.24 = bf16[1,1,1408,2048]{3,2,1,0:T(8,128)(2,1)} fusion(bf16[192,1408]{1,0:T(8,128)(2,1)} %copy-done.22, bf16[192,2048]{1,0:T(8,128)(2,1)} %reshape.238), kind=kOutput, calls=%fused_computation.38 | convolution fusion | flops 1110179840 | bytes 7094272 | tf_op jit(solution)/shard_map/dot_general | solution.py:39
  148.6 4.2 %fusion.23 = bf16[1,1,1408,2048]{3,2,1,0:T(8,128)(2,1)} fusion(bf16[192,1408]{1,0:T(8,128)(2,1)S(1)} %copy-done.24, bf16[192,2048]{1,0:T(8,128)(2,1)S(1)} %copy-done.7), kind=kOutput, calls=%fused_computation.37 | convolution fusion | flops 1110179840 | bytes 7094272 | tf_op jit(solution)/shard_map/dot_general | solution.py:36
  152.9 4.3 %fusion.25 = bf16[1,1,1408,2048]{3,2,1,0:T(8,128)(2,1)} fusion(bf16[192,2048]{1,0:T(8,128)(2,1)S(1)} %copy-done.9, f32[192,1408]{1,0:T(8,128)S(1)} %copy-done.21, f32[192,1408]{1,0:T(8,128)S(1)} %copy-done.19), kind=kOutput, calls=%fused_computation.39 | convolution fusion | flops 1111801856 | bytes 8716288 | tf_op jit(solution)/shard_map/dot_general | solution.py:40
  157.2 5.5 %all-to-all-done.5 = bf16[8,4,6,2048]{3,1,2,0:T(4,128)(2,1)S(1)} async-done(((bf16[8,4,6,2048]{3,1,2,0:T(4,128)(2,1)}), bf16[8,4,6,2048]{3,1,2,0:T(4,128)(2,1)S(1)}, u32[]{:S(2)}, u32[]{:S(2)}) %all-to-all-start.5) | async-done | bytes 786464 | tf_op jit(solution)/shard_map/all_to_all | solution.py:195
  163.6 31.4 %all_gather.9 = bf16[128,2048]{1,0:T(8,128)(2,1)S(1)} all-gather(bf16[16,2048]{1,0:T(8,128)(2,1)S(1)} %fusion.63), channel_id=1, replica_groups=mesh['ctx'=4,'ep'=8] {'ep'}, dimensions={0}, use_global_device_ids=true | all-gather | bytes 589824 | tf_op jit(solution)/shard_map/all_gather | solution.py:210
  196.6 25.1 %while.22 = (s32[]{:T(128)}, bf16[2,128,2,128]{3,1,2,0:T(8,128)(2,1)S(1)}, f32[128,2,128]{2,0,1:T(8,128)S(1)}, f32[2,2,128]{2,1,0:T(2,128)S(1)}, f32[2,128,2,128...) while((s32[]{:T(128)}, ...), condition=%wide.region_8.9_spmd.clone, body=%wide.region_7.8_spmd.clone.sunk | while | flops 42483984 | bytes 3723668 | solution.py:246
  199.7 2.9 %collective-permute-done.1 = f32[128,2,128]{2,0,1:T(8,128)S(1)} collective-permute-done((f32[128,2,128]{2,0,1:T(8,128)S(1)}, f32[128,2,128]{2,0,1:T(8,128)S(1)}, u32[]{:S(2)}, u32[]{:S(2)}) %collective-permute-start.1) | collective-permute-done | bytes 131104 | tf_op jit(solution)/shard_map/while/body/eval_jaxpr/ppermute | solution.py:17
  202.6 1.5 collective-permute-start
  205.6 3.6 %collective-permute-done.1 = f32[128,2,128]{2,0,1:T(8,128)S(1)} collective-permute-done((f32[128,2,128]{2,0,1:T(8,128)S(1)}, f32[128,2,128]{2,0,1:T(8,128)S(1)}, u32[]{:S(2)}, u32[]{:S(2)}) %collective-permute-start.1) | collective-permute-done | bytes 131104 | tf_op jit(solution)/shard_map/while/body/eval_jaxpr/ppermute | solution.py:17
  212.2 2.9 %collective-permute-done.1 = f32[128,2,128]{2,0,1:T(8,128)S(1)} collective-permute-done((f32[128,2,128]{2,0,1:T(8,128)S(1)}, f32[128,2,128]{2,0,1:T(8,128)S(1)}, u32[]{:S(2)}, u32[]{:S(2)}) %collective-permute-start.1) | collective-permute-done | bytes 131104 | tf_op jit(solution)/shard_map/while/body/eval_jaxpr/ppermute | solution.py:17
  215.1 1.5 collective-permute-start
  218.1 3.6 %collective-permute-done.1 = f32[128,2,128]{2,0,1:T(8,128)S(1)} collective-permute-done((f32[128,2,128]{2,0,1:T(8,128)S(1)}, f32[128,2,128]{2,0,1:T(8,128)S(1)}, u32[]{:S(2)}, u32[]{:S(2)}) %collective-permute-start.1) | collective-permute-done | bytes 131104 | tf_op jit(solution)/shard_map/while/body/eval_jaxpr/ppermute | solution.py:17
  (188 shorter events, 28.2 us)
Async XLA Ops:
  0.6 194.4 %copy-start = (bf16[256,2048]{1,0:T(8,128)(2,1)S(1)}, bf16[256,2048]{1,0:T(8,128)(2,1)}, u32[]{:S(2)}) copy-start(bf16[256,2048]{1,0:T(8,128)(2,1)} %param.22) | copy-start | bytes 3145732
  4.6 8.8 %copy-start.17 = (f32[16,6]{0,1:T(8,128)S(1)}, f32[16,6]{0,1:T(8,128)}, u32[]{:S(2)}) copy-start(f32[16,6]{0,1:T(8,128)} %param.17) | copy-start | bytes 1156
  4.6 9.0 %copy-start.11 = (bf16[16,2048]{1,0:T(8,128)(2,1)S(1)}, bf16[16,2048]{1,0:T(8,128)(2,1)}, u32[]{:S(2)}) copy-start(bf16[16,2048]{1,0:T(8,128)(2,1)} %param.15) | copy-start | bytes 196612
  6.1 27.6 %all-to-all-start.2 = ((bf16[8,4,6,2048]{3,1,2,0:T(4,128)(2,1)}), bf16[8,4,6,2048]{3,1,2,0:T(4,128)(2,1)}, u32[]{:S(2)}, u32[]{:S(2)}) async-start(bf16[8,4,6,2048]{3,1,2,0:T(4,128)(2,1)} %copy.110), calls=%async_computation.2 | async-start | bytes 1572864 | tf_op jit(solution)/shard_map/all_to_all | solution.py:174
  33.6 23.9 %all-to-all-start = ((bf16[8,4,6,2048]{3,1,2,0:T(4,128)(2,1)}), bf16[8,4,6,2048]{3,1,2,0:T(4,128)(2,1)S(1)}, u32[]{:S(2)}, u32[]{:S(2)}) async-start(bf16[8,4,6,2048]{3,1,2,0:T(4,128)(2,1)} %copy.107), calls=%async_computation | async-start | bytes 1572864 | tf_op jit(solution)/shard_map/all_to_all | solution.py:175
  37.2 23.9 %copy-start.2 = (bf16[128,256]{1,0:T(8,128)(2,1)S(1)}, bf16[128,256]{1,0:T(8,128)(2,1)}, u32[]{:S(2)}) copy-start(bf16[128,256]{1,0:T(8,128)(2,1)} %param.24) | copy-start | bytes 196612
  37.2 24.0 %copy-start.1 = (bf16[128,256]{1,0:T(8,128)(2,1)S(1)}, bf16[128,256]{1,0:T(8,128)(2,1)}, u32[]{:S(2)}) copy-start(bf16[128,256]{1,0:T(8,128)(2,1)} %param.25) | copy-start | bytes 196612
  57.6 18.7 %all-to-all-start.3 = ((bf16[8,4,6,2048]{3,0,2,1:T(8,128)(2,1)}), bf16[8,4,6,2048]{3,0,2,1:T(8,128)(2,1)S(1)}, u32[]{:S(2)}, u32[]{:S(2)}) async-start(bf16[8,4,6,2048]{3,0,2,1:T(8,128)(2,1)} %copy.111), calls=%async_computation.3 | async-start | bytes 1572864 | tf_op jit(solution)/shard_map/all_to_all | solution.py:178
  75.0 19.5 %copy-start.10 = (bf16[128,256]{1,0:T(8,128)(2,1)S(1)}, bf16[128,256]{1,0:T(8,128)(2,1)}, u32[]{:S(2)}) copy-start(bf16[128,256]{1,0:T(8,128)(2,1)} %param.23) | copy-start | bytes 196612
  76.3 21.7 %all-to-all-start.1 = ((bf16[8,4,6,2048]{3,0,2,1:T(8,128)(2,1)}), bf16[8,4,6,2048]{3,0,2,1:T(8,128)(2,1)}, u32[]{:S(2)}, u32[]{:S(2)}) async-start(bf16[8,4,6,2048]{3,0,2,1:T(8,128)(2,1)} %copy.108), calls=%async_computation.1 | async-start | bytes 1572864 | tf_op jit(solution)/shard_map/all_to_all | solution.py:179
  105.5 10.5 %slice-start = ((s8[5767168]{0:T(1024)(128)(4,1)}), s8[4194304]{0:T(1024)(128)(4,1)S(1)}, s32[]{:S(2)}) async-start(s8[5767168]{0:T(1024)(128)(4,1)} %bitcast.172), calls=%async_computation.6 | async-start | bytes 8388608
  105.5 12.0 %slice-start.2 = ((s8[5767168]{0:T(1024)(128)(4,1)}), s8[4194304]{0:T(1024)(128)(4,1)S(1)}, s32[]{:S(2)}) async-start(s8[5767168]{0:T(1024)(128)(4,1)} %bitcast.174), calls=%async_computation.8 | async-start | bytes 8388608
  122.5 15.1 %all-to-all-start.4 = ((bf16[8,4,6,2048]{3,0,2,1:T(8,128)(2,1)}), bf16[8,4,6,2048]{3,0,2,1:T(8,128)(2,1)S(1)}, u32[]{:S(2)}, u32[]{:S(2)}) async-start(bf16[8,4,6,2048]{3,0,2,1:T(8,128)(2,1)} %copy.113), calls=%async_computation.4 | async-start | bytes 1572864 | tf_op jit(solution)/shard_map/all_to_all | solution.py:188
  126.3 16.6 %copy-start.16 = (s32[16,6]{0,1:T(8,128)S(1)}, s32[16,6]{0,1:T(8,128)}, u32[]{:S(2)}) copy-start(s32[16,6]{0,1:T(8,128)} %param.16) | copy-start | bytes 1156
  139.1 23.6 %all-to-all-start.5 = ((bf16[8,4,6,2048]{3,1,2,0:T(4,128)(2,1)}), bf16[8,4,6,2048]{3,1,2,0:T(4,128)(2,1)S(1)}, u32[]{:S(2)}, u32[]{:S(2)}) async-start(bf16[8,4,6,2048]{3,1,2,0:T(4,128)(2,1)} %copy.114), calls=%async_computation.5 | async-start | bytes 1572864 | tf_op jit(solution)/shard_map/all_to_all | solution.py:195
  152.9 10.5 %copy-start.5 = (bf16[16,2048]{1,0:T(8,128)(2,1)S(1)}, bf16[16,2048]{1,0:T(8,128)(2,1)}, u32[]{:S(2)}) copy-start(bf16[16,2048]{1,0:T(8,128)(2,1)} %param.14) | copy-start | bytes 196612
  152.9 10.5 %copy-start.15 = (f32[2048]{0:T(1024)S(1)}, f32[2048]{0:T(1024)}, u32[]{:S(2)}) copy-start(f32[2048]{0:T(1024)} %param.18) | copy-start | bytes 24580
  152.9 10.6 %copy-start.12 = (bf16[16,2048]{1,0:T(8,128)(2,1)S(1)}, bf16[16,2048]{1,0:T(8,128)(2,1)}, u32[]{:S(2)}) copy-start(bf16[16,2048]{1,0:T(8,128)(2,1)} %param.15) | copy-start | bytes 196612
  163.4 32.4 %copy-start.14 = (bf16[128,256]{0,1:T(8,128)(2,1)S(1)}, bf16[128,256]{0,1:T(8,128)(2,1)}, u32[]{:S(2)}) copy-start(bf16[128,256]{0,1:T(8,128)(2,1)} %copy.116) | copy-start | bytes 196612
  163.6 32.3 %copy-start.13 = (bf16[16,2048]{1,0:T(8,128)(2,1)}, bf16[16,2048]{1,0:T(8,128)(2,1)S(1)}, u32[]{:S(2)}) copy-start(bf16[16,2048]{1,0:T(8,128)(2,1)S(1)} %fusion.63) | copy-start | bytes 196612
  196.6 3.1 %collective-permute-start.2 = (f32[2,2,128]{2,1,0:T(2,128)S(1)}, f32[2,2,128]{2,1,0:T(2,128)S(1)}, u32[]{:S(2)}, u32[]{:S(2)}) collective-permute-start(f32[2,2,128]{2,1,0:T(2,128)S(1)} %copy.187), channel_id=1, source_target_pairs={{24,0},{0,8},{8,16},{16,24},{25,1},{1,9},{9,17},{17,25},{26,2},{2,... | collective-permute-start | bytes 6152 | tf_op jit(solution)/shard_map/while/body/eval_jaxpr/ppermute | solution.py:17
  196.7 5.9 %collective-permute-start = (bf16[2,128,2,128]{3,1,2,0:T(8,128)(2,1)S(1)}, bf16[2,128,2,128]{3,1,2,0:T(8,128)(2,1)S(1)}, u32[]{:S(2)}, u32[]{:S(2)}) collective-permute-start(bf16[2,128,2,128]{3,1,2,0:T(8,128)(2,1)S(1)} %copy.185), channel_id=1, source_target_pairs={{24,0},{0,8},{8,16},{16,24},{25,1},{1,9},{9,17},{17,25},{26,2},{2,... | collective-permute-start | bytes 393224 | tf_op jit(solution)/shard_map/while/body/eval_jaxpr/ppermute | solution.py:17
  198.1 4.5 %collective-permute-start.1 = (f32[128,2,128]{2,0,1:T(8,128)S(1)}, f32[128,2,128]{2,0,1:T(8,128)S(1)}, u32[]{:S(2)}, u32[]{:S(2)}) collective-permute-start(f32[128,2,128]{2,0,1:T(8,128)S(1)} %fusion.130), channel_id=1, source_target_pairs={{24,0},{0,8},{8,16},{16,24},{25,1},{1,9},{9,17},{17,25},{26,2},{2,... | collective-permute-start | bytes 393224 | tf_op jit(solution)/shard_map/while/body/eval_jaxpr/ppermute | solution.py:17
  202.5 3.0 %collective-permute-start.2 = (f32[2,2,128]{2,1,0:T(2,128)S(1)}, f32[2,2,128]{2,1,0:T(2,128)S(1)}, u32[]{:S(2)}, u32[]{:S(2)}) collective-permute-start(f32[2,2,128]{2,1,0:T(2,128)S(1)} %copy.187), channel_id=1, source_target_pairs={{24,0},{0,8},{8,16},{16,24},{25,1},{1,9},{9,17},{17,25},{26,2},{2,... | collective-permute-start | bytes 6152 | tf_op jit(solution)/shard_map/while/body/eval_jaxpr/ppermute | solution.py:17
  202.6 6.6 %collective-permute-start = (bf16[2,128,2,128]{3,1,2,0:T(8,128)(2,1)S(1)}, bf16[2,128,2,128]{3,1,2,0:T(8,128)(2,1)S(1)}, u32[]{:S(2)}, u32[]{:S(2)}) collective-permute-start(bf16[2,128,2,128]{3,1,2,0:T(8,128)(2,1)S(1)} %copy.185), channel_id=1, source_target_pairs={{24,0},{0,8},{8,16},{16,24},{25,1},{1,9},{9,17},{17,25},{26,2},{2,... | collective-permute-start | bytes 393224 | tf_op jit(solution)/shard_map/while/body/eval_jaxpr/ppermute | solution.py:17
  204.7 4.4 %collective-permute-start.1 = (f32[128,2,128]{2,0,1:T(8,128)S(1)}, f32[128,2,128]{2,0,1:T(8,128)S(1)}, u32[]{:S(2)}, u32[]{:S(2)}) collective-permute-start(f32[128,2,128]{2,0,1:T(8,128)S(1)} %fusion.130), channel_id=1, source_target_pairs={{24,0},{0,8},{8,16},{16,24},{25,1},{1,9},{9,17},{17,25},{26,2},{2,... | collective-permute-start | bytes 393224 | tf_op jit(solution)/shard_map/while/body/eval_jaxpr/ppermute | solution.py:17
  209.2 3.0 %collective-permute-start.2 = (f32[2,2,128]{2,1,0:T(2,128)S(1)}, f32[2,2,128]{2,1,0:T(2,128)S(1)}, u32[]{:S(2)}, u32[]{:S(2)}) collective-permute-start(f32[2,2,128]{2,1,0:T(2,128)S(1)} %copy.187), channel_id=1, source_target_pairs={{24,0},{0,8},{8,16},{16,24},{25,1},{1,9},{9,17},{17,25},{26,2},{2,... | collective-permute-start | bytes 6152 | tf_op jit(solution)/shard_map/while/body/eval_jaxpr/ppermute | solution.py:17
  209.2 5.9 %collective-permute-start = (bf16[2,128,2,128]{3,1,2,0:T(8,128)(2,1)S(1)}, bf16[2,128,2,128]{3,1,2,0:T(8,128)(2,1)S(1)}, u32[]{:S(2)}, u32[]{:S(2)}) collective-permute-start(bf16[2,128,2,128]{3,1,2,0:T(8,128)(2,1)S(1)} %copy.185), channel_id=1, source_target_pairs={{24,0},{0,8},{8,16},{16,24},{25,1},{1,9},{9,17},{17,25},{26,2},{2,... | collective-permute-start | bytes 393224 | tf_op jit(solution)/shard_map/while/body/eval_jaxpr/ppermute | solution.py:17
  210.6 4.4 %collective-permute-start.1 = (f32[128,2,128]{2,0,1:T(8,128)S(1)}, f32[128,2,128]{2,0,1:T(8,128)S(1)}, u32[]{:S(2)}, u32[]{:S(2)}) collective-permute-start(f32[128,2,128]{2,0,1:T(8,128)S(1)} %fusion.130), channel_id=1, source_target_pairs={{24,0},{0,8},{8,16},{16,24},{25,1},{1,9},{9,17},{17,25},{26,2},{2,... | collective-permute-start | bytes 393224 | tf_op jit(solution)/shard_map/while/body/eval_jaxpr/ppermute | solution.py:17
  215.1 3.0 %collective-permute-start.2 = (f32[2,2,128]{2,1,0:T(2,128)S(1)}, f32[2,2,128]{2,1,0:T(2,128)S(1)}, u32[]{:S(2)}, u32[]{:S(2)}) collective-permute-start(f32[2,2,128]{2,1,0:T(2,128)S(1)} %copy.187), channel_id=1, source_target_pairs={{24,0},{0,8},{8,16},{16,24},{25,1},{1,9},{9,17},{17,25},{26,2},{2,... | collective-permute-start | bytes 6152 | tf_op jit(solution)/shard_map/while/body/eval_jaxpr/ppermute | solution.py:17
  215.1 6.6 %collective-permute-start = (bf16[2,128,2,128]{3,1,2,0:T(8,128)(2,1)S(1)}, bf16[2,128,2,128]{3,1,2,0:T(8,128)(2,1)S(1)}, u32[]{:S(2)}, u32[]{:S(2)}) collective-permute-start(bf16[2,128,2,128]{3,1,2,0:T(8,128)(2,1)S(1)} %copy.185), channel_id=1, source_target_pairs={{24,0},{0,8},{8,16},{16,24},{25,1},{1,9},{9,17},{17,25},{26,2},{2,... | collective-permute-start | bytes 393224 | tf_op jit(solution)/shard_map/while/body/eval_jaxpr/ppermute | solution.py:17
  217.2 4.4 %collective-permute-start.1 = (f32[128,2,128]{2,0,1:T(8,128)S(1)}, f32[128,2,128]{2,0,1:T(8,128)S(1)}, u32[]{:S(2)}, u32[]{:S(2)}) collective-permute-start(f32[128,2,128]{2,0,1:T(8,128)S(1)} %fusion.130), channel_id=1, source_target_pairs={{24,0},{0,8},{8,16},{16,24},{25,1},{1,9},{9,17},{17,25},{26,2},{2,... | collective-permute-start | bytes 393224 | tf_op jit(solution)/shard_map/while/body/eval_jaxpr/ppermute | solution.py:17
  (15 other events, 63.5 us)
where the time goes:
time: 224 us; the launch traced here: 223 us
  waiting for transfers between devices  67.9 us (30%)
  blocking collectives  58.9 us (26%)
  matrix products  40.1 us (18%)
  starting transfers between devices  31 us (14%)
  local copies, waits for them, and re-layouts  19.2 us (9%)
  other arithmetic  4.58 us (2%)
    all_gather x1, blocking collectives, local(): lax.all_gather(grad_state, 'ep', axis=0, tiled=True)  31.4 us
    all_to_all x1, waiting for transfers between devices, local(): lax.all_to_all(send_rows, 'ep', split_axis=0, concat_axis=0, tiled=True)  17.9 us
    all_to_all x1, waiting for transfers between devices, local(): lax.all_to_all(send_grads, 'ep', split_axis=0, concat_axis=0, tiled=True)  17.9 us
    ppermute x12, waiting for transfers between devices, shifted(): return lax.ppermute(block, axis, route)  15.2 us
    all_gather x1, blocking collectives, local(): lax.all_gather(key_rows, 'ctx', axis=0, tiled=True)  13.9 us
    all_gather x1, blocking collectives, local(): lax.all_gather(value_rows, 'ctx', axis=0, tiled=True)  13.6 us
    all_to_all x1, waiting for transfers between devices, local(): lax.all_to_all(partial_value.reshape(ep_count, ctx_count, capacity, model...  11.3 us
    all_to_all x1, starting transfers between devices, local(): lax.all_to_all(send_rows, 'ep', split_axis=0, concat_axis=0, tiled=True)  7.28 us
  transfers between devices with their start and end apart: 18, of which 12 were waited for; matrix products, arithmetic and copies ran while one was open for 13% of the time, Pallas kernels for 0%

commit v1 on v0

--- a/solution.py
+++ b/solution.py
@@ -185,13 +185,12 @@
         up_w,
         down_w,
     )
-    returned = lax.all_to_all(
-        partial_value.reshape(ep_count, ctx_count, capacity, model_width),
-        "ctx",
-        split_axis=1,
-        concat_axis=1,
-        tiled=True,
-    )
+    body = partial_value.reshape(ep_count, ctx_count, capacity, model_width)
+    answer = lax.axis_size("ctx")
+    then = jnp.split(body, answer, 1)
+    val = jnp.stack(then, 0)
+    near = lax.all_to_all(val, "ctx", 0, 0)
+    returned = jnp.concatenate(near, 1)
     returned = lax.all_to_all(returned, "ep", split_axis=0, concat_axis=0, tiled=True)
     summed = jnp.sum(
         returned.reshape(ep_count, EXP_DEV, copies, capacity, model_width).astype(jnp.float32),

time: 224 us -> 222 us (level)
  no operation moved by 1% of the time
where the time goes in v1:
time: 222 us
  waiting for transfers between devices  67.9 us (31%)
  blocking collectives  58.9 us (27%)
  matrix products  39.2 us (18%)
  starting transfers between devices  31 us (14%)
  local copies, waits for them, and re-layouts  18.2 us (8%)
  other arithmetic  4.86 us (2%)
    all_gather x1, blocking collectives, local(): lax.all_gather(grad_state, 'ep', axis=0, tiled=True)  31.4 us
    all_to_all x1, waiting for transfers between devices, local(): lax.all_to_all(send_rows, 'ep', split_axis=0, concat_axis=0, tiled=True)  17.9 us
    all_to_all x1, waiting for transfers between devices, local(): lax.all_to_all(send_grads, 'ep', split_axis=0, concat_axis=0, tiled=True)  17.9 us
    ppermute x12, waiting for transfers between devices, shifted(): return lax.ppermute(block, axis, route)  15.2 us
    all_gather x1, blocking collectives, local(): lax.all_gather(key_rows, 'ctx', axis=0, tiled=True)  13.9 us
    all_gather x1, blocking collectives, local(): lax.all_gather(value_rows, 'ctx', axis=0, tiled=True)  13.6 us
    all_to_all x1, waiting for transfers between devices, local(): near = lax.all_to_all(val, 'ctx', 0, 0)  11.3 us
    all_to_all x1, starting transfers between devices, local(): lax.all_to_all(send_rows, 'ep', split_axis=0, concat_axis=0, tiled=True)  7.28 us
  transfers between devices with their start and end apart: 18, of which 12 were waited for; matrix products, arithmetic and copies ran while one was open for 13% of the time, Pallas kernels for 0%

profile of v1, /device:TPU:0, one launch (start us, length us, event | category | flops | bytes accessed | tf_op | source)
XLA Modules:
  0.0 221.6 jit_solution(6095270176135750106)
XLA Ops:
  4.6 1.5 copy.122
  6.1 7.3 %all-to-all-start.2 = ((bf16[8,4,6,2048]{3,1,2,0:T(4,128)(2,1)}), bf16[8,4,6,2048]{3,1,2,0:T(4,128)(2,1)}, u32[]{:S(2)}, u32[]{:S(2)}) async-start(bf16[8,4,6,2048]{3,1,2,0:T(4,128)(2,1)} %copy.122), calls=%async_computation.2 | async-start | bytes 1572864 | tf_op jit(solution)/shard_map/all_to_all | solution.py:174
  14.2 1.5 copy.119
  15.7 17.9 %all-to-all-done.2 = bf16[8,4,6,2048]{3,1,2,0:T(4,128)(2,1)} async-done(((bf16[8,4,6,2048]{3,1,2,0:T(4,128)(2,1)}), bf16[8,4,6,2048]{3,1,2,0:T(4,128)(2,1)}, u32[]{:S(2)}, u32[]{:S(2)}) %all-to-all-start.2) | async-done | bytes 786464 | tf_op jit(solution)/shard_map/all_to_all | solution.py:174
  33.6 3.6 %all-to-all-start = ((bf16[8,4,6,2048]{3,1,2,0:T(4,128)(2,1)}), bf16[8,4,6,2048]{3,1,2,0:T(4,128)(2,1)S(1)}, u32[]{:S(2)}, u32[]{:S(2)}) async-start(bf16[8,4,6,2048]{3,1,2,0:T(4,128)(2,1)} %copy.119), calls=%async_computation | async-start | bytes 1572864 | tf_op jit(solution)/shard_map/all_to_all | solution.py:175
  37.2 2.5 %copy.123 = bf16[8,4,6,2048]{3,0,2,1:T(8,128)(2,1)} copy(bf16[8,4,6,2048]{3,1,2,0:T(4,128)(2,1)} %all-to-all-done.2) | data formatting | bytes 1572864 | tf_op jit(solution)/shard_map/all_to_all | solution.py:174
  39.7 17.9 %all-to-all-done = bf16[8,4,6,2048]{3,1,2,0:T(4,128)(2,1)S(1)} async-done(((bf16[8,4,6,2048]{3,1,2,0:T(4,128)(2,1)}), bf16[8,4,6,2048]{3,1,2,0:T(4,128)(2,1)S(1)}, u32[]{:S(2)}, u32[]{:S(2)}) %all-to-all-start) | async-done | bytes 786464 | tf_op jit(solution)/shard_map/all_to_all | solution.py:175
  57.6 3.5 %all-to-all-start.3 = ((bf16[8,4,6,2048]{3,0,2,1:T(8,128)(2,1)}), bf16[8,4,6,2048]{3,0,2,1:T(8,128)(2,1)S(1)}, u32[]{:S(2)}, u32[]{:S(2)}) async-start(bf16[8,4,6,2048]{3,0,2,1:T(8,128)(2,1)} %copy.123), calls=%async_computation.3 | async-start | bytes 1572864 | tf_op jit(solution)/shard_map/all_to_all | solution.py:178
  61.4 13.6 %all_gather.11 = bf16[512,256]{0,1:T(8,128)(2,1)S(1)} all-gather(bf16[128,256]{0,1:T(8,128)(2,1)S(1)} %copy.136), channel_id=1, replica_groups=mesh['ctx'=4,'ep'=8] {'ctx'}, dimensions={0}, use_global_device_ids=true | all-gather | bytes 327680 | tf_op jit(solution)/shard_map/all_gather | solution.py:134
  76.3 4.2 %all-to-all-start.1 = ((bf16[8,4,6,2048]{3,0,2,1:T(8,128)(2,1)}), bf16[8,4,6,2048]{3,0,2,1:T(8,128)(2,1)}, u32[]{:S(2)}, u32[]{:S(2)}) async-start(bf16[8,4,6,2048]{3,0,2,1:T(8,128)(2,1)} %copy.120), calls=%async_computation.1 | async-start | bytes 1572864 | tf_op jit(solution)/shard_map/all_to_all | solution.py:179
  80.5 13.9 %all_gather.10 = bf16[512,256]{0,1:T(8,128)(2,1)S(1)} all-gather(bf16[128,256]{0,1:T(8,128)(2,1)S(1)} %copy.133), channel_id=1, replica_groups=mesh['ctx'=4,'ep'=8] {'ctx'}, dimensions={0}, use_global_device_ids=true | all-gather | bytes 327680 | tf_op jit(solution)/shard_map/all_gather | solution.py:133
  98.0 1.6 copy.121
  100.8 4.7 %fusion.28 = f32[192,1408]{1,0:T(8,128)S(1)} fusion(bf16[192,2048]{1,0:T(8,128)(2,1)S(1)} %copy-done.6, bf16[1,1,1408,2048]{3,2,1,0:T(8,128)(2,1)} %param.19), kind=kOutput, calls=%fused_computation.42 | convolution fusion | flops 1107296256 | bytes 7634944 | tf_op jit(solution)/shard_map/dot_general | solution.py:23
  105.5 5.1 %fusion.32 = f32[192,1408]{1,0:T(8,128)S(1)} fusion(bf16[192,2048]{1,0:T(8,128)(2,1)S(1)} %copy-done.6, bf16[1,1,1408,2048]{3,2,1,0:T(8,128)(2,1)} %param.20), kind=kOutput, calls=%fused_computation.46 | convolution fusion | flops 1107296256 | bytes 7634944 | tf_op jit(solution)/shard_map/dot_general | solution.py:24
  110.7 5.3 %multiply_convert_fusion.1 = (bf16[192,1408]{1,0:T(8,128)(2,1)S(1)}, bf16[192,1408]{1,0:T(8,128)(2,1)S(1)}) fusion(f32[192,1408]{1,0:T(8,128)S(1)} %fusion.28, f32[192,1408]{1,0:T(8,128)S(1)} %fusion.32, bf16[192,2048]{1,0:T(8,128)(2,1)S(1)} %copy-done.8, bf16[1,1,1408,2048]{3,2,1,0:T(8,128)(2,1)} %param.21), kind=kOutput, calls=%fused_computation.62 | convolution fusion | flops 1110810624 | bytes 9797632 | tf_op jit(solution)/shard_map/dot_general | solution.py:27
  117.5 1.4 fusion.39
  120.9 3.5 %all-to-all-start.4 = ((bf16[4,8,1,6,2048]{4,1,3,2,0:T(8,128)(2,1)}), bf16[4,8,1,6,2048]{4,1,3,2,0:T(8,128)(2,1)S(1)}, u32[]{:S(2)}, u32[]{:S(2)}) async-start(bf16[4,8,1,6,2048]{4,1,3,2,0:T(8,128)(2,1)} %copy.128), calls=%async_computation.4 | async-start | bytes 1572864 | tf_op jit(solution)/shard_map/all_to_all | solution.py:192
  124.7 11.3 %all-to-all-done.4 = bf16[4,8,1,6,2048]{4,1,3,2,0:T(8,128)(2,1)S(1)} async-done(((bf16[4,8,1,6,2048]{4,1,3,2,0:T(8,128)(2,1)}), bf16[4,8,1,6,2048]{4,1,3,2,0:T(8,128)(2,1)S(1)}, u32[]{:S(2)}, u32[]{:S(2)}) %all-to-all-start.4) | async-done | bytes 786464 | tf_op jit(solution)/shard_map/all_to_all | solution.py:192
  136.0 1.5 copy.129
  137.5 3.8 %all-to-all-start.5 = ((bf16[8,4,6,2048]{3,1,2,0:T(4,128)(2,1)}), bf16[8,4,6,2048]{3,1,2,0:T(4,128)(2,1)S(1)}, u32[]{:S(2)}, u32[]{:S(2)}) async-start(bf16[8,4,6,2048]{3,1,2,0:T(4,128)(2,1)} %copy.129), calls=%async_computation.5 | async-start | bytes 1572864 | tf_op jit(solution)/shard_map/all_to_all | solution.py:194
  141.4 5.6 %fusion.24 = bf16[1,1,1408,2048]{3,2,1,0:T(8,128)(2,1)} fusion(bf16[192,1408]{1,0:T(8,128)(2,1)} %copy-done.22, bf16[192,2048]{1,0:T(8,128)(2,1)} %reshape.244), kind=kOutput, calls=%fused_computation.38 | convolution fusion | flops 1110179840 | bytes 7094272 | tf_op jit(solution)/shard_map/dot_general | solution.py:39
  147.0 4.2 %fusion.23 = bf16[1,1,1408,2048]{3,2,1,0:T(8,128)(2,1)} fusion(bf16[192,1408]{1,0:T(8,128)(2,1)S(1)} %copy-done.24, bf16[192,2048]{1,0:T(8,128)(2,1)S(1)} %copy-done.7), kind=kOutput, calls=%fused_computation.37 | convolution fusion | flops 1110179840 | bytes 7094272 | tf_op jit(solution)/shard_map/dot_general | solution.py:36
  151.3 4.3 %fusion.25 = bf16[1,1,1408,2048]{3,2,1,0:T(8,128)(2,1)} fusion(bf16[192,2048]{1,0:T(8,128)(2,1)S(1)} %copy-done.9, f32[192,1408]{1,0:T(8,128)S(1)} %copy-done.21, f32[192,1408]{1,0:T(8,128)S(1)} %copy-done.19), kind=kOutput, calls=%fused_computation.39 | convolution fusion | flops 1111801856 | bytes 8716288 | tf_op jit(solution)/shard_map/dot_general | solution.py:40
  155.6 5.5 %all-to-all-done.5 = bf16[8,4,6,2048]{3,1,2,0:T(4,128)(2,1)S(1)} async-done(((bf16[8,4,6,2048]{3,1,2,0:T(4,128)(2,1)}), bf16[8,4,6,2048]{3,1,2,0:T(4,128)(2,1)S(1)}, u32[]{:S(2)}, u32[]{:S(2)}) %all-to-all-start.5) | async-done | bytes 786464 | tf_op jit(solution)/shard_map/all_to_all | solution.py:194
  162.1 31.4 %all_gather.9 = bf16[128,2048]{1,0:T(8,128)(2,1)S(1)} all-gather(bf16[16,2048]{1,0:T(8,128)(2,1)S(1)} %fusion.63), channel_id=1, replica_groups=mesh['ctx'=4,'ep'=8] {'ep'}, dimensions={0}, use_global_device_ids=true | all-gather | bytes 589824 | tf_op jit(solution)/shard_map/all_gather | solution.py:209
  195.0 25.1 %while.22 = (s32[]{:T(128)}, bf16[2,128,2,128]{3,1,2,0:T(8,128)(2,1)S(1)}, f32[128,2,128]{2,0,1:T(8,128)S(1)}, f32[2,2,128]{2,1,0:T(2,128)S(1)}, f32[2,128,2,128...) while((s32[]{:T(128)}, ...), condition=%wide.region_8.9_spmd.clone, body=%wide.region_7.8_spmd.clone.sunk | while | flops 42483984 | bytes 3723668 | solution.py:245
  198.1 2.9 %collective-permute-done.1 = f32[128,2,128]{2,0,1:T(8,128)S(1)} collective-permute-done((f32[128,2,128]{2,0,1:T(8,128)S(1)}, f32[128,2,128]{2,0,1:T(8,128)S(1)}, u32[]{:S(2)}, u32[]{:S(2)}) %collective-permute-start.1) | collective-permute-done | bytes 131104 | tf_op jit(solution)/shard_map/while/body/eval_jaxpr/ppermute | solution.py:17
  201.0 1.5 collective-permute-start
  204.0 3.6 %collective-permute-done.1 = f32[128,2,128]{2,0,1:T(8,128)S(1)} collective-permute-done((f32[128,2,128]{2,0,1:T(8,128)S(1)}, f32[128,2,128]{2,0,1:T(8,128)S(1)}, u32[]{:S(2)}, u32[]{:S(2)}) %collective-permute-start.1) | collective-permute-done | bytes 131104 | tf_op jit(solution)/shard_map/while/body/eval_jaxpr/ppermute | solution.py:17
  210.6 2.9 %collective-permute-done.1 = f32[128,2,128]{2,0,1:T(8,128)S(1)} collective-permute-done((f32[128,2,128]{2,0,1:T(8,128)S(1)}, f32[128,2,128]{2,0,1:T(8,128)S(1)}, u32[]{:S(2)}, u32[]{:S(2)}) %collective-permute-start.1) | collective-permute-done | bytes 131104 | tf_op jit(solution)/shard_map/while/body/eval_jaxpr/ppermute | solution.py:17
  213.5 1.5 collective-permute-start
  216.5 3.6 %collective-permute-done.1 = f32[128,2,128]{2,0,1:T(8,128)S(1)} collective-permute-done((f32[128,2,128]{2,0,1:T(8,128)S(1)}, f32[128,2,128]{2,0,1:T(8,128)S(1)}, u32[]{:S(2)}, u32[]{:S(2)}) %collective-permute-start.1) | collective-permute-done | bytes 131104 | tf_op jit(solution)/shard_map/while/body/eval_jaxpr/ppermute | solution.py:17
  (190 shorter events, 27.5 us)
Async XLA Ops:
  0.6 192.9 %copy-start = (bf16[256,2048]{1,0:T(8,128)(2,1)S(1)}, bf16[256,2048]{1,0:T(8,128)(2,1)}, u32[]{:S(2)}) copy-start(bf16[256,2048]{1,0:T(8,128)(2,1)} %param.22) | copy-start | bytes 3145732
  4.6 8.8 %copy-start.17 = (f32[16,6]{0,1:T(8,128)S(1)}, f32[16,6]{0,1:T(8,128)}, u32[]{:S(2)}) copy-start(f32[16,6]{0,1:T(8,128)} %param.17) | copy-start | bytes 1156
  4.6 9.0 %copy-start.11 = (bf16[16,2048]{1,0:T(8,128)(2,1)S(1)}, bf16[16,2048]{1,0:T(8,128)(2,1)}, u32[]{:S(2)}) copy-start(bf16[16,2048]{1,0:T(8,128)(2,1)} %param.15) | copy-start | bytes 196612
  6.1 27.6 %all-to-all-start.2 = ((bf16[8,4,6,2048]{3,1,2,0:T(4,128)(2,1)}), bf16[8,4,6,2048]{3,1,2,0:T(4,128)(2,1)}, u32[]{:S(2)}, u32[]{:S(2)}) async-start(bf16[8,4,6,2048]{3,1,2,0:T(4,128)(2,1)} %copy.122), calls=%async_computation.2 | async-start | bytes 1572864 | tf_op jit(solution)/shard_map/all_to_all | solution.py:174
  33.6 23.9 %all-to-all-start = ((bf16[8,4,6,2048]{3,1,2,0:T(4,128)(2,1)}), bf16[8,4,6,2048]{3,1,2,0:T(4,128)(2,1)S(1)}, u32[]{:S(2)}, u32[]{:S(2)}) async-start(bf16[8,4,6,2048]{3,1,2,0:T(4,128)(2,1)} %copy.119), calls=%async_computation | async-start | bytes 1572864 | tf_op jit(solution)/shard_map/all_to_all | solution.py:175
  37.2 23.9 %copy-start.2 = (bf16[128,256]{1,0:T(8,128)(2,1)S(1)}, bf16[128,256]{1,0:T(8,128)(2,1)}, u32[]{:S(2)}) copy-start(bf16[128,256]{1,0:T(8,128)(2,1)} %param.24) | copy-start | bytes 196612
  37.2 24.0 %copy-start.1 = (bf16[128,256]{1,0:T(8,128)(2,1)S(1)}, bf16[128,256]{1,0:T(8,128)(2,1)}, u32[]{:S(2)}) copy-start(bf16[128,256]{1,0:T(8,128)(2,1)} %param.25) | copy-start | bytes 196612
  57.6 18.7 %all-to-all-start.3 = ((bf16[8,4,6,2048]{3,0,2,1:T(8,128)(2,1)}), bf16[8,4,6,2048]{3,0,2,1:T(8,128)(2,1)S(1)}, u32[]{:S(2)}, u32[]{:S(2)}) async-start(bf16[8,4,6,2048]{3,0,2,1:T(8,128)(2,1)} %copy.123), calls=%async_computation.3 | async-start | bytes 1572864 | tf_op jit(solution)/shard_map/all_to_all | solution.py:178
  75.0 19.5 %copy-start.10 = (bf16[128,256]{1,0:T(8,128)(2,1)S(1)}, bf16[128,256]{1,0:T(8,128)(2,1)}, u32[]{:S(2)}) copy-start(bf16[128,256]{1,0:T(8,128)(2,1)} %param.23) | copy-start | bytes 196612
  76.3 21.7 %all-to-all-start.1 = ((bf16[8,4,6,2048]{3,0,2,1:T(8,128)(2,1)}), bf16[8,4,6,2048]{3,0,2,1:T(8,128)(2,1)}, u32[]{:S(2)}, u32[]{:S(2)}) async-start(bf16[8,4,6,2048]{3,0,2,1:T(8,128)(2,1)} %copy.120), calls=%async_computation.1 | async-start | bytes 1572864 | tf_op jit(solution)/shard_map/all_to_all | solution.py:179
  105.5 10.5 %slice-start = ((s8[5767168]{0:T(1024)(128)(4,1)}), s8[4194304]{0:T(1024)(128)(4,1)S(1)}, s32[]{:S(2)}) async-start(s8[5767168]{0:T(1024)(128)(4,1)} %bitcast.190), calls=%async_computation.6 | async-start | bytes 8388608
  105.5 12.0 %slice-start.2 = ((s8[5767168]{0:T(1024)(128)(4,1)}), s8[4194304]{0:T(1024)(128)(4,1)S(1)}, s32[]{:S(2)}) async-start(s8[5767168]{0:T(1024)(128)(4,1)} %bitcast.192), calls=%async_computation.8 | async-start | bytes 8388608
  110.7 6.8 %slice-start.3 = ((s8[5767168]{0:T(1024)(128)(4,1)}), s8[1572864]{0:T(1024)(128)(4,1)S(1)}, s32[]{:S(2)}) async-start(s8[5767168]{0:T(1024)(128)(4,1)} %bitcast.192), calls=%async_computation.9 | async-start | bytes 3145728
  120.9 15.1 %all-to-all-start.4 = ((bf16[4,8,1,6,2048]{4,1,3,2,0:T(8,128)(2,1)}), bf16[4,8,1,6,2048]{4,1,3,2,0:T(8,128)(2,1)S(1)}, u32[]{:S(2)}, u32[]{:S(2)}) async-start(bf16[4,8,1,6,2048]{4,1,3,2,0:T(8,128)(2,1)} %copy.128), calls=%async_computation.4 | async-start | bytes 1572864 | tf_op jit(solution)/shard_map/all_to_all | solution.py:192
  137.5 23.6 %all-to-all-start.5 = ((bf16[8,4,6,2048]{3,1,2,0:T(4,128)(2,1)}), bf16[8,4,6,2048]{3,1,2,0:T(4,128)(2,1)S(1)}, u32[]{:S(2)}, u32[]{:S(2)}) async-start(bf16[8,4,6,2048]{3,1,2,0:T(4,128)(2,1)} %copy.129), calls=%async_computation.5 | async-start | bytes 1572864 | tf_op jit(solution)/shard_map/all_to_all | solution.py:194
  151.3 10.5 %copy-start.5 = (bf16[16,2048]{1,0:T(8,128)(2,1)S(1)}, bf16[16,2048]{1,0:T(8,128)(2,1)}, u32[]{:S(2)}) copy-start(bf16[16,2048]{1,0:T(8,128)(2,1)} %param.14) | copy-start | bytes 196612
  151.3 10.5 %copy-start.15 = (f32[2048]{0:T(1024)S(1)}, f32[2048]{0:T(1024)}, u32[]{:S(2)}) copy-start(f32[2048]{0:T(1024)} %param.18) | copy-start | bytes 24580
  151.3 10.6 %copy-start.12 = (bf16[16,2048]{1,0:T(8,128)(2,1)S(1)}, bf16[16,2048]{1,0:T(8,128)(2,1)}, u32[]{:S(2)}) copy-start(bf16[16,2048]{1,0:T(8,128)(2,1)} %param.15) | copy-start | bytes 196612
  161.8 32.4 %copy-start.14 = (bf16[128,256]{0,1:T(8,128)(2,1)S(1)}, bf16[128,256]{0,1:T(8,128)(2,1)}, u32[]{:S(2)}) copy-start(bf16[128,256]{0,1:T(8,128)(2,1)} %copy.131) | copy-start | bytes 196612
  162.1 32.3 %copy-start.13 = (bf16[16,2048]{1,0:T(8,128)(2,1)}, bf16[16,2048]{1,0:T(8,128)(2,1)S(1)}, u32[]{:S(2)}) copy-start(bf16[16,2048]{1,0:T(8,128)(2,1)S(1)} %fusion.63) | copy-start | bytes 196612
  195.0 3.1 %collective-permute-start.2 = (f32[2,2,128]{2,1,0:T(2,128)S(1)}, f32[2,2,128]{2,1,0:T(2,128)S(1)}, u32[]{:S(2)}, u32[]{:S(2)}) collective-permute-start(f32[2,2,128]{2,1,0:T(2,128)S(1)} %copy.205), channel_id=1, source_target_pairs={{24,0},{0,8},{8,16},{16,24},{25,1},{1,9},{9,17},{17,25},{26,2},{2,... | collective-permute-start | bytes 6152 | tf_op jit(solution)/shard_map/while/body/eval_jaxpr/ppermute | solution.py:17
  195.1 5.9 %collective-permute-start = (bf16[2,128,2,128]{3,1,2,0:T(8,128)(2,1)S(1)}, bf16[2,128,2,128]{3,1,2,0:T(8,128)(2,1)S(1)}, u32[]{:S(2)}, u32[]{:S(2)}) collective-permute-start(bf16[2,128,2,128]{3,1,2,0:T(8,128)(2,1)S(1)} %copy.203), channel_id=1, source_target_pairs={{24,0},{0,8},{8,16},{16,24},{25,1},{1,9},{9,17},{17,25},{26,2},{2,... | collective-permute-start | bytes 393224 | tf_op jit(solution)/shard_map/while/body/eval_jaxpr/ppermute | solution.py:17
  196.5 4.5 %collective-permute-start.1 = (f32[128,2,128]{2,0,1:T(8,128)S(1)}, f32[128,2,128]{2,0,1:T(8,128)S(1)}, u32[]{:S(2)}, u32[]{:S(2)}) collective-permute-start(f32[128,2,128]{2,0,1:T(8,128)S(1)} %fusion.130), channel_id=1, source_target_pairs={{24,0},{0,8},{8,16},{16,24},{25,1},{1,9},{9,17},{17,25},{26,2},{2,... | collective-permute-start | bytes 393224 | tf_op jit(solution)/shard_map/while/body/eval_jaxpr/ppermute | solution.py:17
  201.0 3.0 %collective-permute-start.2 = (f32[2,2,128]{2,1,0:T(2,128)S(1)}, f32[2,2,128]{2,1,0:T(2,128)S(1)}, u32[]{:S(2)}, u32[]{:S(2)}) collective-permute-start(f32[2,2,128]{2,1,0:T(2,128)S(1)} %copy.205), channel_id=1, source_target_pairs={{24,0},{0,8},{8,16},{16,24},{25,1},{1,9},{9,17},{17,25},{26,2},{2,... | collective-permute-start | bytes 6152 | tf_op jit(solution)/shard_map/while/body/eval_jaxpr/ppermute | solution.py:17
  201.0 6.6 %collective-permute-start = (bf16[2,128,2,128]{3,1,2,0:T(8,128)(2,1)S(1)}, bf16[2,128,2,128]{3,1,2,0:T(8,128)(2,1)S(1)}, u32[]{:S(2)}, u32[]{:S(2)}) collective-permute-start(bf16[2,128,2,128]{3,1,2,0:T(8,128)(2,1)S(1)} %copy.203), channel_id=1, source_target_pairs={{24,0},{0,8},{8,16},{16,24},{25,1},{1,9},{9,17},{17,25},{26,2},{2,... | collective-permute-start | bytes 393224 | tf_op jit(solution)/shard_map/while/body/eval_jaxpr/ppermute | solution.py:17
  203.1 4.4 %collective-permute-start.1 = (f32[128,2,128]{2,0,1:T(8,128)S(1)}, f32[128,2,128]{2,0,1:T(8,128)S(1)}, u32[]{:S(2)}, u32[]{:S(2)}) collective-permute-start(f32[128,2,128]{2,0,1:T(8,128)S(1)} %fusion.130), channel_id=1, source_target_pairs={{24,0},{0,8},{8,16},{16,24},{25,1},{1,9},{9,17},{17,25},{26,2},{2,... | collective-permute-start | bytes 393224 | tf_op jit(solution)/shard_map/while/body/eval_jaxpr/ppermute | solution.py:17
  207.6 3.0 %collective-permute-start.2 = (f32[2,2,128]{2,1,0:T(2,128)S(1)}, f32[2,2,128]{2,1,0:T(2,128)S(1)}, u32[]{:S(2)}, u32[]{:S(2)}) collective-permute-start(f32[2,2,128]{2,1,0:T(2,128)S(1)} %copy.205), channel_id=1, source_target_pairs={{24,0},{0,8},{8,16},{16,24},{25,1},{1,9},{9,17},{17,25},{26,2},{2,... | collective-permute-start | bytes 6152 | tf_op jit(solution)/shard_map/while/body/eval_jaxpr/ppermute | solution.py:17
  207.6 5.9 %collective-permute-start = (bf16[2,128,2,128]{3,1,2,0:T(8,128)(2,1)S(1)}, bf16[2,128,2,128]{3,1,2,0:T(8,128)(2,1)S(1)}, u32[]{:S(2)}, u32[]{:S(2)}) collective-permute-start(bf16[2,128,2,128]{3,1,2,0:T(8,128)(2,1)S(1)} %copy.203), channel_id=1, source_target_pairs={{24,0},{0,8},{8,16},{16,24},{25,1},{1,9},{9,17},{17,25},{26,2},{2,... | collective-permute-start | bytes 393224 | tf_op jit(solution)/shard_map/while/body/eval_jaxpr/ppermute | solution.py:17
  209.0 4.4 %collective-permute-start.1 = (f32[128,2,128]{2,0,1:T(8,128)S(1)}, f32[128,2,128]{2,0,1:T(8,128)S(1)}, u32[]{:S(2)}, u32[]{:S(2)}) collective-permute-start(f32[128,2,128]{2,0,1:T(8,128)S(1)} %fusion.130), channel_id=1, source_target_pairs={{24,0},{0,8},{8,16},{16,24},{25,1},{1,9},{9,17},{17,25},{26,2},{2,... | collective-permute-start | bytes 393224 | tf_op jit(solution)/shard_map/while/body/eval_jaxpr/ppermute | solution.py:17
  213.5 3.0 %collective-permute-start.2 = (f32[2,2,128]{2,1,0:T(2,128)S(1)}, f32[2,2,128]{2,1,0:T(2,128)S(1)}, u32[]{:S(2)}, u32[]{:S(2)}) collective-permute-start(f32[2,2,128]{2,1,0:T(2,128)S(1)} %copy.205), channel_id=1, source_target_pairs={{24,0},{0,8},{8,16},{16,24},{25,1},{1,9},{9,17},{17,25},{26,2},{2,... | collective-permute-start | bytes 6152 | tf_op jit(solution)/shard_map/while/body/eval_jaxpr/ppermute | solution.py:17
  213.5 6.6 %collective-permute-start = (bf16[2,128,2,128]{3,1,2,0:T(8,128)(2,1)S(1)}, bf16[2,128,2,128]{3,1,2,0:T(8,128)(2,1)S(1)}, u32[]{:S(2)}, u32[]{:S(2)}) collective-permute-start(bf16[2,128,2,128]{3,1,2,0:T(8,128)(2,1)S(1)} %copy.203), channel_id=1, source_target_pairs={{24,0},{0,8},{8,16},{16,24},{25,1},{1,9},{9,17},{17,25},{26,2},{2,... | collective-permute-start | bytes 393224 | tf_op jit(solution)/shard_map/while/body/eval_jaxpr/ppermute | solution.py:17
  215.6 4.4 %collective-permute-start.1 = (f32[128,2,128]{2,0,1:T(8,128)S(1)}, f32[128,2,128]{2,0,1:T(8,128)S(1)}, u32[]{:S(2)}, u32[]{:S(2)}) collective-permute-start(f32[128,2,128]{2,0,1:T(8,128)S(1)} %fusion.130), channel_id=1, source_target_pairs={{24,0},{0,8},{8,16},{16,24},{25,1},{1,9},{9,17},{17,25},{26,2},{2,... | collective-permute-start | bytes 393224 | tf_op jit(solution)/shard_map/while/body/eval_jaxpr/ppermute | solution.py:17
  (15 other events, 61.9 us)
